TPU v7x, 128 devices: a whole 4x4x4 slice. The times are simulated.
128 devices in a mesh: lon: 16 (over y_hi, z, core), lat: 8 (over y_lo, x).
Axes of the slice: x: 4, y: 4 (y_hi: 2, y_lo: 2; y = y_hi * 2 + y_lo), z: 4, core: 2. Of those that a mesh axis runs over, the one named last changes fastest.
Arguments:
- temp_before: float32 [25, 512, 2048], P(None, 'lat', 'lon'), may hold values from -8 to 8
- temp_now: float32 [25, 512, 2048], P(None, 'lat', 'lon'), may hold values from -8 to 8
- salt_before: float32 [25, 512, 2048], P(None, 'lat', 'lon'), may hold values from -4 to 4
- salt_now: float32 [25, 512, 2048], P(None, 'lat', 'lon'), may hold values from -4 to 4
- east_velocity: float32 [25, 512, 2048], P(None, 'lat', 'lon'), may hold values from -0.3 to 0.3, as said below
- north_velocity: float32 [25, 512, 2048], P(None, 'lat', 'lon'), may hold values from -0.3 to 0.3, as said below
- bottom_level: int32 [512, 2048], P('lat', 'lon'), may hold values from 0 to 25, as said below
Outputs:
- temp_out: float32 [25, 512, 2048], P(None, 'lat', 'lon')
- salt_out: float32 [25, 512, 2048], P(None, 'lat', 'lon')
- density_out: float32 [25, 512, 2048], P(None, 'lat', 'lon')
Inputs may be any that keep to these rules, and one draw needn't show every extreme that they name: `bottom_level`: cells at levels below a column's value are ocean, the others land; every column of row 0 is land. `east_velocity`: zero on every face that touches a land cell; the face east of column 2047 touches column 0. `north_velocity`: zero on every face that touches a land cell; on row 511 the north face of column i touches cell (511, 2047 - i) and carries the negative of that column's value.
All inputs are finite; a program needn't handle non-finite values.
Results may differ from a plain program's by a relative error of at most 0.00002.
Values sent between devices are 32-bit elements; how exact they have to be, the bound alone decides.
No kernel may reach another device: no remote copies, remote signals or barrier semaphores. Data moves between devices by JAX's collectives and lax.ppermute only.
A program may use at most 256 MiB of HBM per device.

v0:
```python
import jax
import jax.numpy as jnp
from jax import lax
from jax.sharding import PartitionSpec as P

asselin_gamma = 0.1
nu_base = 0.05
nu_conv = 0.2
level_depth = 160.0
alpha_zero = 0.1655
beta_zero = 0.76554
lambda_one = 0.05952
lambda_two = 0.00054914
mu_one = 0.0001497
mu_two = 1.109e-05
nu_cross = 0.0024341


def extended_2(value, sides, width, wrap):
    for axis, dim in sides:
        count, length = (lax.axis_size(axis), value.shape[dim])
        up = [(i, (i + 1) % count) for i in range(count if wrap else count - 1)]
        down = [(j, i) for i, j in up]
        last = lax.slice_in_dim(value, length - width, length, axis=dim)
        leading = lax.slice_in_dim(value, 0, width, axis=dim)
        before = lax.ppermute(last, axis, up)
        after = lax.ppermute(leading, axis, down)
        value = jnp.concatenate([before, value, after], axis=dim)
    return value


def passed_along(block, axis, distance):
    devices = range(lax.axis_size(axis))
    route = [((i - distance) % len(devices), i) for i in devices]
    return lax.ppermute(block, axis, route)


def from_behind(value, axis, by):
    count = lax.axis_size(axis)
    pairs = [(i, i + by) for i in range(count) if 0 <= i + by < count]
    return lax.ppermute(value, axis, pairs)


def density(temp, salt):
    depth = level_depth * (jnp.arange(temp.shape[0], dtype=jnp.float32) + 0.5)[:, None, None]
    warm = -alpha_zero * (1.0 + 0.5 * lambda_one * temp + mu_one * depth) * temp
    salty = beta_zero * (1.0 - 0.5 * lambda_two * salt - mu_two * depth) * salt
    return warm + salty - nu_cross * temp * salt


def divergence(extended, velocity, along):
    face_count = velocity.shape[along - 1]
    behind_far = lax.slice_in_dim(extended, 0, face_count, axis=along)
    behind = lax.slice_in_dim(extended, 1, face_count + 1, axis=along)
    ahead = lax.slice_in_dim(extended, 2, face_count + 2, axis=along)
    ahead_far = lax.slice_in_dim(extended, 3, face_count + 3, axis=along)
    flux = velocity * (7.0 * (behind + ahead) - (behind_far + ahead_far)) / 12.0
    flux = flux + jnp.abs(velocity) * (ahead_far - behind_far - 3.0 * (ahead - behind)) / 12.0
    return lax.slice_in_dim(flux, 1, face_count, axis=along) - lax.slice_in_dim(
        flux, 0, face_count - 1, axis=along
    )


def vertical_mixing(before, now, ocean_mask):
    density_now = density(now[0], now[1])
    density_jump = density_now[1:] - density_now[:-1]
    mixing_rates = (nu_base + nu_conv * jax.nn.sigmoid(-4.0 * density_jump)) * ocean_mask[1:]
    flux = mixing_rates * (before[:, 1:] - before[:, :-1])
    padding = jnp.zeros_like(flux[:, :1])
    return jnp.concatenate([flux, padding], 1) - jnp.concatenate([padding, flux], 1)


def advance(before, now, x_ext, y_ext, east_faces, north_faces, ocean_mask):
    change = -(divergence(x_ext, east_faces, 3) + divergence(y_ext, north_faces, 2))
    change = change + vertical_mixing(before, now, ocean_mask)
    after = (before + 2.0 * change) * ocean_mask
    filtered = now + asselin_gamma * (before - 2.0 * now + after)
    return (filtered, after)


def extend_tracers(now, at_fold, columns):
    x_ext = extended_2(now, (("lon", 3),), 2, True)
    y_part = extended_2(now, (("lat", 2),), 2, False)
    edge_rows = now[:, :, -2:, :]
    cycle_size = lax.axis_size("lon")
    pieces = edge_rows.reshape(
        edge_rows.shape[0], edge_rows.shape[1], 2, cycle_size, columns // cycle_size
    )
    spread = lax.all_to_all(pieces, "lon", split_axis=3, concat_axis=3, tiled=True)
    returned = lax.all_to_all(
        spread[:, :, :, ::-1, :], "lon", split_axis=3, concat_axis=3, tiled=True
    )
    partner_rows = returned.reshape(edge_rows.shape)
    mirror = partner_rows[:, :, ::-1, ::-1]
    north_rows = jnp.where(at_fold, mirror, y_part[:, :, -2:, :])
    y_ext = jnp.concatenate([y_part[:, :, :-2, :], north_rows], 2)
    return (x_ext, y_ext)


def on_device(
    temp_before, temp_now, salt_before, salt_now, east_velocity, north_velocity, bottom_level
):
    levels = temp_now.shape[0]
    columns = temp_now.shape[2]
    ocean_mask = (jnp.arange(levels, dtype=jnp.int32)[:, None, None] < bottom_level[None]).astype(
        jnp.float32
    )
    before = jnp.stack([temp_before, salt_before]) * ocean_mask
    now = jnp.stack([temp_now, salt_now]) * ocean_mask
    west_column = passed_along(east_velocity[:, :, -1:], "lon", 1)
    east_faces = jnp.concatenate([west_column, east_velocity], 2)
    south_row = from_behind(north_velocity[:, -1:, :], "lat", 1)
    north_faces = jnp.concatenate([south_row, north_velocity], 1)
    at_fold = lax.axis_index("lat") == lax.axis_size("lat") - 1
    for step_index in range(2):
        x_ext, y_ext = extend_tracers(now, at_fold, columns)
        before, now = advance(before, now, x_ext, y_ext, east_faces, north_faces, ocean_mask)
    final_density = density(now[0], now[1]) * ocean_mask
    return (now[0], now[1], final_density)


def solution(mesh):
    return jax.shard_map(
        on_device,
        mesh=mesh,
        in_specs=(
            P(None, "lat", "lon"),
            P(None, "lat", "lon"),
            P(None, "lat", "lon"),
            P(None, "lat", "lon"),
            P(None, "lat", "lon"),
            P(None, "lat", "lon"),
            P("lat", "lon"),
        ),
        out_specs=(P(None, "lat", "lon"), P(None, "lat", "lon"), P(None, "lat", "lon")),
        check_vma=False,
    )
```

profile of v0, /device:TPU:25, one launch (start us, length us, event | category | flops | bytes accessed | tf_op | source)
XLA Modules:
  0.0 146.9 jit_solution(7164898051214208194)
XLA Ops:
  0.7 1.6 %slice.173 = f32[25,1,128]{2,1,0:T(1,128)} slice(f32[25,64,128]{2,1,0:T(8,128)} %param.12), slice={[0:25], [63:64], [0:128]} | slice | bytes 25600 | tf_op jit(solution)/shard_map/slice | solution.py:112
  2.2 3.1 %collective-permute-start.3 = (f32[25,1,128]{2,1,0:T(1,128)}, f32[25,1,128]{2,1,0:T(1,128)}, u32[]{:S(2)}, u32[]{:S(2)}) collective-permute-start(f32[25,1,128]{2,1,0:T(1,128)} %slice.173), channel_id=1, source_target_pairs={{0,1},{1,2},{2,3},{3,4},{4,5},{5,6},{6,7},{8,9},{9,10},{10,11},{11... | collective-permute-start | bytes 38408 | tf_op jit(solution)/shard_map/ppermute | solution.py:41
  5.3 1.4 slice.164
  7.1 2.5 %collective-permute-start = (f32[25,64,1]{1,0,2:T(8,128)S(1)}, f32[25,64,1]{1,0,2:T(8,128)}, u32[]{:S(2)}, u32[]{:S(2)}) collective-permute-start(f32[25,64,1]{1,0,2:T(8,128)S(1)} %copy.111), channel_id=1, source_target_pairs={{120,0},{0,8},{8,16},{16,24},{24,32},{32,40},{40,48},{48,56},{56,6... | collective-permute-start | bytes 19208 | tf_op jit(solution)/shard_map/ppermute | solution.py:35
  9.8 3.6 %maximum_multiply_fusion.1 = (f32[2,25,64,128]{3,2,1,0:T(8,128)}, f32[2,25,64,128]{3,2,1,0:T(8,128)S(1)}) fusion(f32[1,25,64,128]{3,2,1,0:T(8,128)S(1)} %bitcast.54, f32[1,25,64,128]{3,2,1,0:T(8,128)} %bitcast.55, f32[25,64,128]{2,1,0:T(8,128)S(1)} %fusion.14, f32[1,25,64,128]{3,2,1,0:T(8,128)} %bitcast.56, f32[1,25,64,128]{3,2,1,0:T(8,128)} %bitcast.57), kind=kLoop, calls=%fused_computation.37 | loop fusion | flops 1638400 | bytes 7372800 | tf_op jit(solution)/shard_map/mul | solution.py:108
  14.1 4.3 %collective-permute-start.5 = (f32[2,25,2,128]{3,2,1,0:T(2,128)}, f32[2,25,2,128]{3,2,1,0:T(2,128)}, u32[]{:S(2)}, u32[]{:S(2)}) collective-permute-start(f32[2,25,2,128]{3,2,1,0:T(2,128)} %get-tuple-element.25), channel_id=1, source_target_pairs={{1,0},{2,1},{3,2},{4,3},{5,4},{6,5},{7,6},{9,8},{10,9},{11,10},{12... | collective-permute-start | bytes 153608 | tf_op jit(solution)/shard_map/ppermute | solution.py:27
  18.4 1.9 %collective-permute-start.4 = (f32[2,25,2,128]{3,2,1,0:T(2,128)}, f32[2,25,2,128]{3,2,1,0:T(2,128)}, u32[]{:S(2)}, u32[]{:S(2)}) collective-permute-start(f32[2,25,2,128]{3,2,1,0:T(2,128)} %get-tuple-element.26), channel_id=1, source_target_pairs={{0,1},{1,2},{2,3},{3,4},{4,5},{5,6},{6,7},{8,9},{9,10},{10,11},{11... | collective-permute-start | bytes 153608 | tf_op jit(solution)/shard_map/ppermute | solution.py:26
  20.3 0.9 copy.99
  21.3 0.9 reshape.71
  22.2 7.6 %all-to-all-start = ((f32[16,1,800]{2,1,0:T(1,128)}), f32[16,1,800]{2,1,0:T(1,128)S(1)}, u32[]{:S(2)}, u32[]{:S(2)}) async-start(f32[16,1,800]{2,1,0:T(1,128)} %reshape.71), calls=%async_computation | async-start | bytes 114688 | tf_op jit(solution)/shard_map/all_to_all | solution.py:89
  29.7 2.3 %fusion.34 = (f32[2,25,64,2]{3,2,1,0:T(8,128)}, f32[2,25,64,2]{3,2,1,0:T(8,128)}) fusion(f32[2,25,64,128]{3,2,1,0:T(8,128)S(1)} %get-tuple-element.30), kind=kLoop, calls=%fused_computation.83 | loop fusion | bytes 102400 | tf_op jit(solution)/shard_map/slice | solution.py:25
  32.0 2.0 %copy.95 = f32[2,25,64,2]{2,3,1,0:T(2,128)S(1)} copy(f32[2,25,64,2]{3,2,1,0:T(8,128)} %get-tuple-element.24) | data formatting | bytes 51200 | tf_op jit(solution)/shard_map/slice | solution.py:24
  34.0 1.5 %collective-permute-start.1 = (f32[2,25,64,2]{2,3,1,0:T(2,128)S(1)}, f32[2,25,64,2]{2,3,1,0:T(2,128)S(1)}, u32[]{:S(2)}, u32[]{:S(2)}) collective-permute-start(f32[2,25,64,2]{2,3,1,0:T(2,128)S(1)} %copy.95), channel_id=1, source_target_pairs={{0,8},{8,16},{16,24},{24,32},{32,40},{40,48},{48,56},{56,64},{64,7... | collective-permute-start | bytes 76808 | tf_op jit(solution)/shard_map/ppermute | solution.py:26
  36.2 1.2 copy-done.3
  37.3 1.5 fusion.13
  40.0 1.9 %copy.94 = f32[25,64,1]{2,1,0:T(8,128)} copy(f32[25,64,1]{1,0,2:T(8,128)} %collective-permute-done) | data formatting | bytes 12800 | tf_op jit(solution)/shard_map/ppermute | solution.py:35
  41.9 3.1 %pad_maximum_fusion.8 = (f32[25,64,129]{2,1,0:T(8,128)S(1)}, f32[25,64,129]{2,1,0:T(8,128)}) fusion(f32[25,64,128]{2,1,0:T(8,128)} %param.11, f32[25,64,1]{2,1,0:T(8,128)} %copy.94), kind=kLoop, calls=%fused_computation.38 | loop fusion | flops 412800 | bytes 2476800 | tf_op jit(solution)/shard_map/concatenate | solution.py:111
  45.1 2.1 %pad_maximum_fusion.9 = (f32[25,65,128]{2,1,0:T(8,128)}, f32[25,65,128]{2,1,0:T(8,128)}) fusion(f32[25,64,128]{2,1,0:T(8,128)S(1)} %copy-done.12, f32[25,1,128]{2,1,0:T(1,128)} %collective-permute-done.3), kind=kLoop, calls=%fused_computation.44 | loop fusion | flops 416000 | bytes 2496000 | tf_op jit(solution)/shard_map/concatenate | solution.py:113
  47.2 1.7 %copy.98 = f32[2,25,64,2]{3,2,1,0:T(8,128)} copy(f32[2,25,64,2]{2,3,1,0:T(2,128)S(1)} %collective-permute-done.2) | data formatting | bytes 51200 | tf_op jit(solution)/shard_map/ppermute | solution.py:27
  48.9 1.8 %copy.96 = f32[2,25,64,2]{3,2,1,0:T(8,128)} copy(f32[2,25,64,2]{2,3,1,0:T(2,128)S(1)} %collective-permute-done.1) | data formatting | bytes 51200 | tf_op jit(solution)/shard_map/ppermute | solution.py:26
  51.2 1.4 reduce
  52.6 1.1 reshape.72
  54.4 1.8 %reshape.73 = f32[16,1,800]{2,1,0:T(1,128)} reshape(f32[16,2,2,8,25]{4,3,2,1,0:T(8,128)} %reverse_bitcast_fusion.1) | data formatting | bytes 102400
  56.2 8.7 %all-to-all-start.1 = ((f32[16,1,800]{2,1,0:T(1,128)}), f32[16,1,800]{2,1,0:T(1,128)S(1)}, u32[]{:S(2)}, u32[]{:S(2)}) async-start(f32[16,1,800]{2,1,0:T(1,128)} %reshape.73), calls=%async_computation.1 | async-start | bytes 114688 | tf_op jit(solution)/shard_map/all_to_all | solution.py:90
  65.0 7.0 %add_multiply_fusion.1 = f32[2,25,64,129]{3,2,1,0:T(8,128)} fusion(f32[2,25,64,128]{3,2,1,0:T(8,128)S(1)} %get-tuple-element.30, f32[2,25,64,2]{3,2,1,0:T(8,128)} %copy.96, f32[2,25,64,2]{3,2,1,0:T(8,128)} %copy.98, f32[25,64,129]{2,1,0:T(8,128)} %get-tuple-element.22, f32[25,64,129]{2,1,0:T(8,128)S(1)} %get-tuple-element.21), kind=kLoop, calls=%fused_computation.9 | loop fusion | flops 6604800 | bytes 4992000 | tf_op jit(solution)/shard_map/add | solution.py:58
  73.5 0.8 broadcast_select_fusion.1
  74.4 2.6 %add_multiply_fusion.3 = f32[2,25,65,128]{3,2,1,0:T(8,128)S(1)} fusion(f32[2,25,64,128]{3,2,1,0:T(8,128)S(1)} %get-tuple-element.30, f32[2,25,2,128]{3,2,1,0:T(2,128)} %collective-permute-done.4, f32[2,25,2,128]{3,2,1,0:T(2,128)S(1)} %broadcast_select_fusion.1, f32[25,65,128]{2,1,0:T(8,128)} %get-tuple-element.28, f32[25,65,128]{2,1,0:T(8,128)S(1)} %copy-done.8), kind=kLoop, calls=%fused_computation.19 | loop fusion | flops 6656000 | bytes 5068800 | tf_op jit(solution)/shard_map/add | solution.py:58
  77.0 5.1 %multiply_add_fusion = (f32[2,25,64,128]{3,2,1,0:T(8,128)}, f32[2,25,64,128]{3,2,1,0:T(8,128)S(1)}) fusion(f32[2,25,64,128]{3,2,1,0:T(8,128)S(1)} %get-tuple-element.30, f32[2,25,64,128]{3,2,1,0:T(8,128)S(1)} %copy-done.4, f32[25,64,128]{2,1,0:T(8,128)S(1)} %copy-done.1, f32[2,24,64,128]{3,2,1,0:T(8,128)S(1)} %copy-done.10, ...), kind=kLoop, calls=%fused_computation.39 | loop fusion | flops 5734400 | bytes 15499264 | tf_op jit(solution)/shard_map/add | solution.py:77
  82.8 2.2 %collective-permute-start.8 = (f32[2,25,2,128]{3,2,1,0:T(2,128)}, f32[2,25,2,128]{3,2,1,0:T(2,128)}, u32[]{:S(2)}, u32[]{:S(2)}) collective-permute-start(f32[2,25,2,128]{3,2,1,0:T(2,128)} %get-tuple-element.20), channel_id=1, source_target_pairs={{0,1},{1,2},{2,3},{3,4},{4,5},{5,6},{6,7},{8,9},{9,10},{10,11},{11... | collective-permute-start | bytes 153608 | tf_op jit(solution)/shard_map/ppermute | solution.py:26
  85.0 0.9 copy.107
  86.4 2.3 %fusion.32 = (f32[2,25,64,2]{3,2,1,0:T(8,128)}, f32[2,25,64,2]{3,2,1,0:T(8,128)}) fusion(f32[2,25,64,128]{3,2,1,0:T(8,128)S(1)} %get-tuple-element.16), kind=kLoop, calls=%fused_computation.81 | loop fusion | bytes 102400 | tf_op jit(solution)/shard_map/slice | solution.py:25
  88.7 5.2 %collective-permute-start.9 = (f32[2,25,2,128]{3,2,1,0:T(2,128)}, f32[2,25,2,128]{3,2,1,0:T(2,128)}, u32[]{:S(2)}, u32[]{:S(2)}) collective-permute-start(f32[2,25,2,128]{3,2,1,0:T(2,128)} %get-tuple-element.19), channel_id=1, source_target_pairs={{1,0},{2,1},{3,2},{4,3},{5,4},{6,5},{7,6},{9,8},{10,9},{11,10},{12... | collective-permute-start | bytes 153608 | tf_op jit(solution)/shard_map/ppermute | solution.py:27
  94.6 1.8 %reshape.75 = f32[16,1,800]{2,1,0:T(1,128)} reshape(f32[16,2,2,8,25]{4,3,2,1,0:T(8,128)} %copy_bitcast_fusion.2) | data formatting | bytes 102400
  96.4 7.8 %all-to-all-start.2 = ((f32[16,1,800]{2,1,0:T(1,128)}), f32[16,1,800]{2,1,0:T(1,128)S(1)}, u32[]{:S(2)}, u32[]{:S(2)}) async-start(f32[16,1,800]{2,1,0:T(1,128)} %reshape.75), calls=%async_computation.2 | async-start | bytes 114688 | tf_op jit(solution)/shard_map/all_to_all | solution.py:89
  104.2 1.1 add_multiply_fusion.4
  105.3 2.1 %copy.105 = f32[2,25,64,2]{2,3,1,0:T(2,128)S(1)} copy(f32[2,25,64,2]{3,2,1,0:T(8,128)} %get-tuple-element.17) | data formatting | bytes 51200 | tf_op jit(solution)/shard_map/slice | solution.py:25
  107.4 2.0 %copy.103 = f32[2,25,64,2]{2,3,1,0:T(2,128)S(1)} copy(f32[2,25,64,2]{3,2,1,0:T(8,128)} %get-tuple-element.18) | data formatting | bytes 51200 | tf_op jit(solution)/shard_map/slice | solution.py:24
  109.4 1.5 %collective-permute-start.6 = (f32[2,25,64,2]{2,3,1,0:T(2,128)S(1)}, f32[2,25,64,2]{2,3,1,0:T(2,128)S(1)}, u32[]{:S(2)}, u32[]{:S(2)}) collective-permute-start(f32[2,25,64,2]{2,3,1,0:T(2,128)S(1)} %copy.103), channel_id=1, source_target_pairs={{0,8},{8,16},{16,24},{24,32},{32,40},{40,48},{48,56},{56,64},{64,7... | collective-permute-start | bytes 76808 | tf_op jit(solution)/shard_map/ppermute | solution.py:26
  110.9 3.6 %fusion.12 = f32[2,24,64,128]{3,2,1,0:T(8,128)} fusion(f32[2,25,64,128]{3,2,1,0:T(8,128)} %get-tuple-element.15, f32[24,64,128]{2,1,0:T(8,128)S(1)} %copy-done.11), kind=kLoop, calls=%fused_computation.41 | loop fusion | flops 786432 | bytes 5505024 | tf_op jit(solution)/shard_map/mul | solution.py:68
  114.7 1.7 %copy.106 = f32[2,25,64,2]{3,2,1,0:T(8,128)} copy(f32[2,25,64,2]{2,3,1,0:T(2,128)S(1)} %collective-permute-done.7) | data formatting | bytes 51200 | tf_op jit(solution)/shard_map/ppermute | solution.py:27
  116.5 1.8 %copy.104 = f32[2,25,64,2]{3,2,1,0:T(8,128)} copy(f32[2,25,64,2]{2,3,1,0:T(2,128)S(1)} %collective-permute-done.6) | data formatting | bytes 51200 | tf_op jit(solution)/shard_map/ppermute | solution.py:26
  119.3 0.9 reshape.77
  120.2 9.1 %all-to-all-start.3 = ((f32[16,1,800]{2,1,0:T(1,128)}), f32[16,1,800]{2,1,0:T(1,128)S(1)}, u32[]{:S(2)}, u32[]{:S(2)}) async-start(f32[16,1,800]{2,1,0:T(1,128)} %reshape.77), calls=%async_computation.3 | async-start | bytes 114688 | tf_op jit(solution)/shard_map/all_to_all | solution.py:90
  129.2 7.2 %add_multiply_fusion = f32[2,25,64,129]{3,2,1,0:T(8,128)} fusion(f32[2,25,64,128]{3,2,1,0:T(8,128)S(1)} %get-tuple-element.16, f32[2,25,64,2]{3,2,1,0:T(8,128)} %copy.104, f32[2,25,64,2]{3,2,1,0:T(8,128)} %copy.106, f32[25,64,129]{2,1,0:T(8,128)} %get-tuple-element.22, f32[25,64,129]{2,1,0:T(8,128)} %copy-done.6), kind=kLoop, calls=%fused_computation.8 | loop fusion | flops 6604800 | bytes 4992000 | tf_op jit(solution)/shard_map/add | solution.py:58
  137.9 0.8 broadcast_select_fusion
  138.8 2.7 %add_multiply_fusion.2 = f32[2,25,65,128]{3,2,1,0:T(8,128)S(1)} fusion(f32[2,25,64,128]{3,2,1,0:T(8,128)S(1)} %get-tuple-element.16, f32[2,25,2,128]{3,2,1,0:T(2,128)} %collective-permute-done.8, f32[2,25,2,128]{3,2,1,0:T(2,128)S(1)} %broadcast_select_fusion, f32[25,65,128]{2,1,0:T(8,128)} %get-tuple-element.28, f32[25,65,128]{2,1,0:T(8,128)} %get-tuple-element.27), kind=kLoop, calls=%fused_computation.18 | loop fusion | flops 6656000 | bytes 5068800 | tf_op jit(solution)/shard_map/add | solution.py:58
  141.8 3.2 %fusion.5 = f32[2,25,64,128]{3,2,1,0:T(8,128)S(1)} fusion(f32[2,25,64,128]{3,2,1,0:T(8,128)S(1)} %copy-done.5, f32[2,25,65,128]{3,2,1,0:T(8,128)S(1)} %add_multiply_fusion.2, f32[2,25,64,129]{3,2,1,0:T(8,128)S(1)} %copy-done.7, f32[2,24,64,128]{3,2,1,0:T(8,128)} %fusion.12, f32[25,64,128]{2,1,0:T(8,128)S(1)} %copy-done.2), kind=kLoop, calls=%fused_computation.26 | loop fusion | flops 3686400 | bytes 12222464 | tf_op jit(solution)/shard_map/mul | solution.py:76
  145.0 1.9 %subtract_select_fusion = (f32[25,64,128]{2,1,0:T(8,128)}, f32[25,64,128]{2,1,0:T(8,128)}, f32[25,64,128]{2,1,0:T(8,128)}) fusion(f32[25]{0:T(128)S(1)} %get-tuple-element.31, f32[25]{0:T(128)S(1)} %get-tuple-element.32, s32[64,128]{1,0:T(8,128)S(1)} %copy-done.15, f32[2,25,64,128]{3,2,1,0:T(8,128)S(1)} %fusion.5), kind=kLoop, calls=%fused_computation.51 | loop fusion | flops 3276800 | bytes 4128968 | tf_op jit(solution)/shard_map/mul | solution.py:118
  (73 shorter events, 10.6 us)
Async XLA Ops:
  0.6 9.0 %copy-start.14 = (s32[64,128]{1,0:T(8,128)S(1)}, s32[64,128]{1,0:T(8,128)}, u32[]{:S(2)}) copy-start(s32[64,128]{1,0:T(8,128)} %param.13) | copy-start | bytes 98308
  0.6 9.1 %copy-start.13 = (f32[25,64,128]{2,1,0:T(8,128)S(1)}, f32[25,64,128]{2,1,0:T(8,128)}, u32[]{:S(2)}) copy-start(f32[25,64,128]{2,1,0:T(8,128)} %param.9) | copy-start | bytes 2457604
  2.2 42.8 %collective-permute-start.3 = (f32[25,1,128]{2,1,0:T(1,128)}, f32[25,1,128]{2,1,0:T(1,128)}, u32[]{:S(2)}, u32[]{:S(2)}) collective-permute-start(f32[25,1,128]{2,1,0:T(1,128)} %slice.173), channel_id=1, source_target_pairs={{0,1},{1,2},{2,3},{3,4},{4,5},{5,6},{6,7},{8,9},{9,10},{10,11},{11... | collective-permute-start | bytes 38408 | tf_op jit(solution)/shard_map/ppermute | solution.py:41
  7.1 32.8 %collective-permute-start = (f32[25,64,1]{1,0,2:T(8,128)S(1)}, f32[25,64,1]{1,0,2:T(8,128)}, u32[]{:S(2)}, u32[]{:S(2)}) collective-permute-start(f32[25,64,1]{1,0,2:T(8,128)S(1)} %copy.111), channel_id=1, source_target_pairs={{120,0},{0,8},{8,16},{16,24},{24,32},{32,40},{40,48},{48,56},{56,6... | collective-permute-start | bytes 19208 | tf_op jit(solution)/shard_map/ppermute | solution.py:35
  9.8 26.1 %copy-start = (f32[25,64,128]{2,1,0:T(8,128)}, f32[25,64,128]{2,1,0:T(8,128)S(1)}, u32[]{:S(2)}) copy-start(f32[25,64,128]{2,1,0:T(8,128)S(1)} %fusion.14) | copy-start | bytes 2457604
  14.1 59.4 %collective-permute-start.5 = (f32[2,25,2,128]{3,2,1,0:T(2,128)}, f32[2,25,2,128]{3,2,1,0:T(2,128)}, u32[]{:S(2)}, u32[]{:S(2)}) collective-permute-start(f32[2,25,2,128]{3,2,1,0:T(2,128)} %get-tuple-element.25), channel_id=1, source_target_pairs={{1,0},{2,1},{3,2},{4,3},{5,4},{6,5},{7,6},{9,8},{10,9},{11,10},{12... | collective-permute-start | bytes 153608 | tf_op jit(solution)/shard_map/ppermute | solution.py:27
  18.4 56.0 %collective-permute-start.4 = (f32[2,25,2,128]{3,2,1,0:T(2,128)}, f32[2,25,2,128]{3,2,1,0:T(2,128)}, u32[]{:S(2)}, u32[]{:S(2)}) collective-permute-start(f32[2,25,2,128]{3,2,1,0:T(2,128)} %get-tuple-element.26), channel_id=1, source_target_pairs={{0,1},{1,2},{2,3},{3,4},{4,5},{5,6},{6,7},{8,9},{9,10},{10,11},{11... | collective-permute-start | bytes 153608 | tf_op jit(solution)/shard_map/ppermute | solution.py:26
  22.2 28.6 %all-to-all-start = ((f32[16,1,800]{2,1,0:T(1,128)}), f32[16,1,800]{2,1,0:T(1,128)S(1)}, u32[]{:S(2)}, u32[]{:S(2)}) async-start(f32[16,1,800]{2,1,0:T(1,128)} %reshape.71), calls=%async_computation | async-start | bytes 114688 | tf_op jit(solution)/shard_map/all_to_all | solution.py:89
  34.0 15.0 %collective-permute-start.1 = (f32[2,25,64,2]{2,3,1,0:T(2,128)S(1)}, f32[2,25,64,2]{2,3,1,0:T(2,128)S(1)}, u32[]{:S(2)}, u32[]{:S(2)}) collective-permute-start(f32[2,25,64,2]{2,3,1,0:T(2,128)S(1)} %copy.95), channel_id=1, source_target_pairs={{0,8},{8,16},{16,24},{24,32},{32,40},{40,48},{48,56},{56,64},{64,7... | collective-permute-start | bytes 76808 | tf_op jit(solution)/shard_map/ppermute | solution.py:26
  35.9 1.4 copy-start.3
  37.3 2.0 %copy-start.9 = (f32[2,25,64,2]{3,2,1,0:T(8,128)S(1)}, f32[2,25,64,2]{3,2,1,0:T(8,128)}, u32[]{:S(2)}) copy-start(f32[2,25,64,2]{3,2,1,0:T(8,128)} %get-tuple-element.23) | copy-start | bytes 76804
  39.9 7.3 %collective-permute-start.2 = (f32[2,25,64,2]{2,3,1,0:T(2,128)S(1)}, f32[2,25,64,2]{2,3,1,0:T(2,128)S(1)}, u32[]{:S(2)}, u32[]{:S(2)}) collective-permute-start(f32[2,25,64,2]{2,3,1,0:T(2,128)S(1)} %copy.97), channel_id=1, source_target_pairs={{8,0},{16,8},{24,16},{32,24},{40,32},{48,40},{56,48},{64,56},{72,6... | collective-permute-start | bytes 76808 | tf_op jit(solution)/shard_map/ppermute | solution.py:27
  41.9 3.1 %copy-start.12 = (f32[25,64,128]{2,1,0:T(8,128)S(1)}, f32[25,64,128]{2,1,0:T(8,128)}, u32[]{:S(2)}) copy-start(f32[25,64,128]{2,1,0:T(8,128)} %param.12) | copy-start | bytes 2457604
  45.1 19.9 %copy-start.6 = (f32[25,64,129]{2,1,0:T(8,128)}, f32[25,64,129]{2,1,0:T(8,128)S(1)}, u32[]{:S(2)}) copy-start(f32[25,64,129]{2,1,0:T(8,128)S(1)} %get-tuple-element.21) | copy-start | bytes 2476804
  56.2 15.7 %all-to-all-start.1 = ((f32[16,1,800]{2,1,0:T(1,128)}), f32[16,1,800]{2,1,0:T(1,128)S(1)}, u32[]{:S(2)}, u32[]{:S(2)}) async-start(f32[16,1,800]{2,1,0:T(1,128)} %reshape.73), calls=%async_computation.1 | async-start | bytes 114688 | tf_op jit(solution)/shard_map/all_to_all | solution.py:90
  72.0 2.4 %copy-start.8 = (f32[25,65,128]{2,1,0:T(8,128)S(1)}, f32[25,65,128]{2,1,0:T(8,128)}, u32[]{:S(2)}) copy-start(f32[25,65,128]{2,1,0:T(8,128)} %get-tuple-element.27) | copy-start | bytes 2496004
  74.4 2.6 %copy-start.1 = (f32[25,64,128]{2,1,0:T(8,128)S(1)}, f32[25,64,128]{2,1,0:T(8,128)}, u32[]{:S(2)}) copy-start(f32[25,64,128]{2,1,0:T(8,128)} %copy-done) | copy-start | bytes 2457604
  74.4 2.6 %copy-start.4 = (f32[2,25,64,128]{3,2,1,0:T(8,128)S(1)}, f32[2,25,64,128]{3,2,1,0:T(8,128)}, u32[]{:S(2)}) copy-start(f32[2,25,64,128]{3,2,1,0:T(8,128)} %get-tuple-element.29) | copy-start | bytes 4915204
  74.4 2.6 %copy-start.10 = (f32[2,24,64,128]{3,2,1,0:T(8,128)S(1)}, f32[2,24,64,128]{3,2,1,0:T(8,128)}, u32[]{:S(2)}) copy-start(f32[2,24,64,128]{3,2,1,0:T(8,128)} %fusion.13) | copy-start | bytes 4718596
  82.8 56.0 %collective-permute-start.8 = (f32[2,25,2,128]{3,2,1,0:T(2,128)}, f32[2,25,2,128]{3,2,1,0:T(2,128)}, u32[]{:S(2)}, u32[]{:S(2)}) collective-permute-start(f32[2,25,2,128]{3,2,1,0:T(2,128)} %get-tuple-element.20), channel_id=1, source_target_pairs={{0,1},{1,2},{2,3},{3,4},{4,5},{5,6},{6,7},{8,9},{9,10},{10,11},{11... | collective-permute-start | bytes 153608 | tf_op jit(solution)/shard_map/ppermute | solution.py:26
  86.4 17.8 %copy-start.2 = (f32[25,64,128]{2,1,0:T(8,128)S(1)}, f32[25,64,128]{2,1,0:T(8,128)}, u32[]{:S(2)}) copy-start(f32[25,64,128]{2,1,0:T(8,128)} %copy-done) | copy-start | bytes 2457604
  88.7 49.3 %collective-permute-start.9 = (f32[2,25,2,128]{3,2,1,0:T(2,128)}, f32[2,25,2,128]{3,2,1,0:T(2,128)}, u32[]{:S(2)}, u32[]{:S(2)}) collective-permute-start(f32[2,25,2,128]{3,2,1,0:T(2,128)} %get-tuple-element.19), channel_id=1, source_target_pairs={{1,0},{2,1},{3,2},{4,3},{5,4},{6,5},{7,6},{9,8},{10,9},{11,10},{12... | collective-permute-start | bytes 153608 | tf_op jit(solution)/shard_map/ppermute | solution.py:27
  96.4 21.9 %all-to-all-start.2 = ((f32[16,1,800]{2,1,0:T(1,128)}), f32[16,1,800]{2,1,0:T(1,128)S(1)}, u32[]{:S(2)}, u32[]{:S(2)}) async-start(f32[16,1,800]{2,1,0:T(1,128)} %reshape.75), calls=%async_computation.2 | async-start | bytes 114688 | tf_op jit(solution)/shard_map/all_to_all | solution.py:89
  105.3 5.6 %copy-start.11 = (f32[24,64,128]{2,1,0:T(8,128)S(1)}, f32[24,64,128]{2,1,0:T(8,128)}, u32[]{:S(2)}) copy-start(f32[24,64,128]{2,1,0:T(8,128)} %add_multiply_fusion.4) | copy-start | bytes 2359300
  109.4 7.1 %collective-permute-start.6 = (f32[2,25,64,2]{2,3,1,0:T(2,128)S(1)}, f32[2,25,64,2]{2,3,1,0:T(2,128)S(1)}, u32[]{:S(2)}, u32[]{:S(2)}) collective-permute-start(f32[2,25,64,2]{2,3,1,0:T(2,128)S(1)} %copy.103), channel_id=1, source_target_pairs={{0,8},{8,16},{16,24},{24,32},{32,40},{40,48},{48,56},{56,64},{64,7... | collective-permute-start | bytes 76808 | tf_op jit(solution)/shard_map/ppermute | solution.py:26
  110.9 3.8 %collective-permute-start.7 = (f32[2,25,64,2]{2,3,1,0:T(2,128)S(1)}, f32[2,25,64,2]{2,3,1,0:T(2,128)S(1)}, u32[]{:S(2)}, u32[]{:S(2)}) collective-permute-start(f32[2,25,64,2]{2,3,1,0:T(2,128)S(1)} %copy.105), channel_id=1, source_target_pairs={{8,0},{16,8},{24,16},{32,24},{40,32},{48,40},{56,48},{64,56},{72,6... | collective-permute-start | bytes 76808 | tf_op jit(solution)/shard_map/ppermute | solution.py:27
  120.2 16.3 %all-to-all-start.3 = ((f32[16,1,800]{2,1,0:T(1,128)}), f32[16,1,800]{2,1,0:T(1,128)S(1)}, u32[]{:S(2)}, u32[]{:S(2)}) async-start(f32[16,1,800]{2,1,0:T(1,128)} %reshape.77), calls=%async_computation.3 | async-start | bytes 114688 | tf_op jit(solution)/shard_map/all_to_all | solution.py:90
  138.8 2.8 %copy-start.5 = (f32[2,25,64,128]{3,2,1,0:T(8,128)S(1)}, f32[2,25,64,128]{3,2,1,0:T(8,128)}, u32[]{:S(2)}) copy-start(f32[2,25,64,128]{3,2,1,0:T(8,128)} %get-tuple-element.15) | copy-start | bytes 4915204
  138.8 3.0 %copy-start.7 = (f32[2,25,64,129]{3,2,1,0:T(8,128)S(1)}, f32[2,25,64,129]{3,2,1,0:T(8,128)}, u32[]{:S(2)}) copy-start(f32[2,25,64,129]{3,2,1,0:T(8,128)} %add_multiply_fusion) | copy-start | bytes 4953604
  141.8 3.2 %copy-start.15 = (s32[64,128]{1,0:T(8,128)S(1)}, s32[64,128]{1,0:T(8,128)}, u32[]{:S(2)}) copy-start(s32[64,128]{1,0:T(8,128)} %param.13) | copy-start | bytes 98308
where the time goes:
time: 148 us; the launch traced here: 147 us
  starting transfers between devices  55.4 us (37%)
  other arithmetic  51.2 us (35%)
  local copies, waits for them, and re-layouts  38.8 us (26%)
    add x4, other arithmetic, divergence(): flux + jnp.abs(velocity) * (ahead_far - behind_far - 3.0 * (ahead - behin...  19.6 us
    all_to_all x2, starting transfers between devices, extend_tracers(): lax.all_to_all(spread[:, :, :, ::-1, :], 'lon', split_axis=3, concat_axis...  17.8 us
    all_to_all x2, starting transfers between devices, extend_tracers(): lax.all_to_all(pieces, 'lon', split_axis=3, concat_axis=3, tiled=True)  15.3 us
    unnamed x45, local copies, waits for them, and re-layouts  11.2 us
    ppermute x4, starting transfers between devices, extended_2(): after = lax.ppermute(leading, axis, down)  9.51 us
    slice x6, local copies, waits for them, and re-layouts, extended_2(): leading = lax.slice_in_dim(value, 0, width, axis=dim)  8.48 us
    ppermute x4, starting transfers between devices, extended_2(): before = lax.ppermute(last, axis, up)  7.17 us
    slice x4, local copies, waits for them, and re-layouts, extended_2(): last = lax.slice_in_dim(value, length - width, length, axis=dim)  5.87 us
  transfers between devices with their start and end apart: 14, of which 1 were waited for; matrix products, arithmetic and copies ran while one was open for 48% of the time, Pallas kernels for 0%

commit v1 on v0

--- a/solution.py
+++ b/solution.py
@@ -86,7 +86,15 @@
     pieces = edge_rows.reshape(
         edge_rows.shape[0], edge_rows.shape[1], 2, cycle_size, columns // cycle_size
     )
-    spread = lax.all_to_all(pieces, "lon", split_axis=3, concat_axis=3, tiled=True)
+    spread = jnp.concatenate(
+        lax.all_to_all(
+            jnp.stack(jnp.split(pieces, lax.psum(1, "lon"), axis=3)),
+            axis_name="lon",
+            split_axis=0,
+            concat_axis=0,
+        ),
+        axis=3,
+    )
     returned = lax.all_to_all(
         spread[:, :, :, ::-1, :], "lon", split_axis=3, concat_axis=3, tiled=True
     )

time: 148 us -> 147 us (level)
  local copies, waits for them, and re-layouts: 38.8 us -> 37.3 us
    unnamed x45 -> x75, local copies, waits for them, and re-layouts: 11.2 us -> 9.61 us
  transfers between devices with their start and end apart: 14 -> 14, of which waited for: 1 -> 1; matrix products, arithmetic and copies ran while one was open for 48% -> 47% of each run, Pallas kernels for 0% -> 0%
where the time goes in v1:
time: 147 us; the launch traced here: 146 us
  starting transfers between devices  55.4 us (38%)
  other arithmetic  51.3 us (35%)
  local copies, waits for them, and re-layouts  37.3 us (25%)
    add x4, other arithmetic, divergence(): flux + jnp.abs(velocity) * (ahead_far - behind_far - 3.0 * (ahead - behin...  19.5 us
    all_to_all x2, starting transfers between devices, extend_tracers(): lax.all_to_all(spread[:, :, :, ::-1, :], 'lon', split_axis=3, concat_axis...  17.8 us
    all_to_all x2, starting transfers between devices, extend_tracers(): lax.all_to_all(jnp.stack(jnp.split(pieces, lax.psum(1, 'lon'), axis=3)),...  15.3 us
    unnamed x75, local copies, waits for them, and re-layouts  9.61 us
    ppermute x4, starting transfers between devices, extended_2(): after = lax.ppermute(leading, axis, down)  9.51 us
    slice x6, local copies, waits for them, and re-layouts, extended_2(): leading = lax.slice_in_dim(value, 0, width, axis=dim)  8.51 us
    ppermute x4, starting transfers between devices, extended_2(): before = lax.ppermute(last, axis, up)  7.17 us
    slice x4, local copies, waits for them, and re-layouts, extended_2(): last = lax.slice_in_dim(value, length - width, length, axis=dim)  5.87 us
  transfers between devices with their start and end apart: 14, of which 1 were waited for; matrix products, arithmetic and copies ran while one was open for 47% of the time, Pallas kernels for 0%

profile of v1, /device:TPU:25, one launch (start us, length us, event | category | flops | bytes accessed | tf_op | source)
XLA Modules:
  0.0 145.7 jit_solution(254289906382361210)
XLA Ops:
  0.7 1.6 %slice.173 = f32[25,1,128]{2,1,0:T(1,128)} slice(f32[25,64,128]{2,1,0:T(8,128)} %param.12), slice={[0:25], [63:64], [0:128]} | slice | bytes 25600 | tf_op jit(solution)/shard_map/slice | solution.py:120
  2.2 3.1 %collective-permute-start.3 = (f32[25,1,128]{2,1,0:T(1,128)}, f32[25,1,128]{2,1,0:T(1,128)}, u32[]{:S(2)}, u32[]{:S(2)}) collective-permute-start(f32[25,1,128]{2,1,0:T(1,128)} %slice.173), channel_id=1, source_target_pairs={{0,1},{1,2},{2,3},{3,4},{4,5},{5,6},{6,7},{8,9},{9,10},{10,11},{11... | collective-permute-start | bytes 38408 | tf_op jit(solution)/shard_map/ppermute | solution.py:41
  5.4 1.4 slice.164
  7.1 2.5 %collective-permute-start = (f32[25,64,1]{1,0,2:T(8,128)S(1)}, f32[25,64,1]{1,0,2:T(8,128)}, u32[]{:S(2)}, u32[]{:S(2)}) collective-permute-start(f32[25,64,1]{1,0,2:T(8,128)S(1)} %copy.287), channel_id=1, source_target_pairs={{120,0},{0,8},{8,16},{16,24},{24,32},{32,40},{40,48},{48,56},{56,6... | collective-permute-start | bytes 19208 | tf_op jit(solution)/shard_map/ppermute | solution.py:35
  9.8 3.7 %maximum_multiply_fusion.1 = (f32[2,25,64,128]{3,2,1,0:T(8,128)}, f32[2,25,64,128]{3,2,1,0:T(8,128)S(1)}) fusion(f32[1,25,64,128]{3,2,1,0:T(8,128)S(1)} %bitcast.276, f32[1,25,64,128]{3,2,1,0:T(8,128)} %bitcast.277, f32[25,64,128]{2,1,0:T(8,128)S(1)} %fusion.14, f32[1,25,64,128]{3,2,1,0:T(8,128)} %bitcast.278, f32[1,25,64,128]{3,2,1,0:T(8,128)} %bitcast.279), kind=kLoop, calls=%fused_computation.37 | loop fusion | flops 1638400 | bytes 7372800 | tf_op jit(solution)/shard_map/mul | solution.py:116
  14.1 4.3 %collective-permute-start.5 = (f32[2,25,2,128]{3,2,1,0:T(2,128)}, f32[2,25,2,128]{3,2,1,0:T(2,128)}, u32[]{:S(2)}, u32[]{:S(2)}) collective-permute-start(f32[2,25,2,128]{3,2,1,0:T(2,128)} %get-tuple-element.25), channel_id=1, source_target_pairs={{1,0},{2,1},{3,2},{4,3},{5,4},{6,5},{7,6},{9,8},{10,9},{11,10},{12... | collective-permute-start | bytes 153608 | tf_op jit(solution)/shard_map/ppermute | solution.py:27
  18.4 1.9 %collective-permute-start.4 = (f32[2,25,2,128]{3,2,1,0:T(2,128)}, f32[2,25,2,128]{3,2,1,0:T(2,128)}, u32[]{:S(2)}, u32[]{:S(2)}) collective-permute-start(f32[2,25,2,128]{3,2,1,0:T(2,128)} %get-tuple-element.26), channel_id=1, source_target_pairs={{0,1},{1,2},{2,3},{3,4},{4,5},{5,6},{6,7},{8,9},{9,10},{10,11},{11... | collective-permute-start | bytes 153608 | tf_op jit(solution)/shard_map/ppermute | solution.py:26
  20.3 0.9 copy.247
  21.5 0.9 reshape.87
  22.3 7.6 %all-to-all-start = ((f32[16,1,800]{2,1,0:T(1,128)}), f32[16,1,800]{2,1,0:T(1,128)S(1)}, u32[]{:S(2)}, u32[]{:S(2)}) async-start(f32[16,1,800]{2,1,0:T(1,128)} %reshape.87), calls=%async_computation | async-start | bytes 114688 | tf_op jit(solution)/shard_map/all_to_all | solution.py:90
  29.9 2.3 %fusion.34 = (f32[2,25,64,2]{3,2,1,0:T(8,128)}, f32[2,25,64,2]{3,2,1,0:T(8,128)}) fusion(f32[2,25,64,128]{3,2,1,0:T(8,128)S(1)} %get-tuple-element.30), kind=kLoop, calls=%fused_computation.147 | loop fusion | bytes 102400 | tf_op jit(solution)/shard_map/slice | solution.py:25
  32.2 2.0 %copy.243 = f32[2,25,64,2]{2,3,1,0:T(2,128)S(1)} copy(f32[2,25,64,2]{3,2,1,0:T(8,128)} %get-tuple-element.24) | data formatting | bytes 51200 | tf_op jit(solution)/shard_map/slice | solution.py:24
  34.2 1.5 %collective-permute-start.1 = (f32[2,25,64,2]{2,3,1,0:T(2,128)S(1)}, f32[2,25,64,2]{2,3,1,0:T(2,128)S(1)}, u32[]{:S(2)}, u32[]{:S(2)}) collective-permute-start(f32[2,25,64,2]{2,3,1,0:T(2,128)S(1)} %copy.243), channel_id=1, source_target_pairs={{0,8},{8,16},{16,24},{24,32},{32,40},{40,48},{48,56},{56,64},{64,7... | collective-permute-start | bytes 76808 | tf_op jit(solution)/shard_map/ppermute | solution.py:26
  36.4 1.2 copy-done.3
  37.5 1.5 %fusion.13 = f32[2,24,64,128]{3,2,1,0:T(8,128)} fusion(f32[2,25,64,128]{3,2,1,0:T(8,128)S(1)} %copy-done.3, f32[24,64,128]{2,1,0:T(8,128)S(1)} %add_multiply_fusion.5), kind=kLoop, calls=%fused_computation.43 | loop fusion | flops 786432 | bytes 5505024 | tf_op jit(solution)/shard_map/mul | solution.py:68
  40.2 1.9 %copy.242 = f32[25,64,1]{2,1,0:T(8,128)} copy(f32[25,64,1]{1,0,2:T(8,128)} %collective-permute-done) | data formatting | bytes 12800 | tf_op jit(solution)/shard_map/ppermute | solution.py:35
  42.1 3.1 %pad_maximum_fusion.8 = (f32[25,64,129]{2,1,0:T(8,128)S(1)}, f32[25,64,129]{2,1,0:T(8,128)}) fusion(f32[25,64,128]{2,1,0:T(8,128)} %param.11, f32[25,64,1]{2,1,0:T(8,128)} %copy.242), kind=kLoop, calls=%fused_computation.38 | loop fusion | flops 412800 | bytes 2476800 | tf_op jit(solution)/shard_map/concatenate | solution.py:119
  45.3 2.1 %pad_maximum_fusion.9 = (f32[25,65,128]{2,1,0:T(8,128)}, f32[25,65,128]{2,1,0:T(8,128)}) fusion(f32[25,64,128]{2,1,0:T(8,128)S(1)} %copy-done.12, f32[25,1,128]{2,1,0:T(1,128)} %collective-permute-done.3), kind=kLoop, calls=%fused_computation.44 | loop fusion | flops 416000 | bytes 2496000 | tf_op jit(solution)/shard_map/concatenate | solution.py:121
  47.4 1.7 %copy.246 = f32[2,25,64,2]{3,2,1,0:T(8,128)} copy(f32[2,25,64,2]{2,3,1,0:T(2,128)S(1)} %collective-permute-done.2) | data formatting | bytes 51200 | tf_op jit(solution)/shard_map/ppermute | solution.py:27
  49.1 1.8 %copy.244 = f32[2,25,64,2]{3,2,1,0:T(8,128)} copy(f32[2,25,64,2]{2,3,1,0:T(2,128)S(1)} %collective-permute-done.1) | data formatting | bytes 51200 | tf_op jit(solution)/shard_map/ppermute | solution.py:26
  51.4 1.4 reduce
  52.8 1.1 reshape.88
  54.0 0.9 reshape.89
  54.8 8.7 %all-to-all-start.1 = ((f32[16,1,800]{2,1,0:T(1,128)}), f32[16,1,800]{2,1,0:T(1,128)S(1)}, u32[]{:S(2)}, u32[]{:S(2)}) async-start(f32[16,1,800]{2,1,0:T(1,128)} %reshape.89), calls=%async_computation.1 | async-start | bytes 114688 | tf_op jit(solution)/shard_map/all_to_all | solution.py:98
  63.6 7.0 %add_multiply_fusion.1 = f32[2,25,64,129]{3,2,1,0:T(8,128)} fusion(f32[2,25,64,128]{3,2,1,0:T(8,128)S(1)} %get-tuple-element.30, f32[2,25,64,2]{3,2,1,0:T(8,128)} %copy.244, f32[2,25,64,2]{3,2,1,0:T(8,128)} %copy.246, f32[25,64,129]{2,1,0:T(8,128)} %get-tuple-element.22, f32[25,64,129]{2,1,0:T(8,128)S(1)} %get-tuple-element.21), kind=kLoop, calls=%fused_computation.9 | loop fusion | flops 6604800 | bytes 4992000 | tf_op jit(solution)/shard_map/add | solution.py:58
  70.5 0.8 reduce.1
  72.1 0.8 broadcast_select_fusion.1
  73.0 2.6 %add_multiply_fusion.3 = f32[2,25,65,128]{3,2,1,0:T(8,128)S(1)} fusion(f32[2,25,64,128]{3,2,1,0:T(8,128)S(1)} %get-tuple-element.30, f32[2,25,2,128]{3,2,1,0:T(2,128)} %collective-permute-done.4, f32[2,25,2,128]{3,2,1,0:T(2,128)S(1)} %broadcast_select_fusion.1, f32[25,65,128]{2,1,0:T(8,128)} %get-tuple-element.28, f32[25,65,128]{2,1,0:T(8,128)S(1)} %copy-done.8), kind=kLoop, calls=%fused_computation.19 | loop fusion | flops 6656000 | bytes 5068800 | tf_op jit(solution)/shard_map/add | solution.py:58
  75.6 5.1 %multiply_add_fusion = (f32[2,25,64,128]{3,2,1,0:T(8,128)}, f32[2,25,64,128]{3,2,1,0:T(8,128)S(1)}) fusion(f32[2,25,64,128]{3,2,1,0:T(8,128)S(1)} %get-tuple-element.30, f32[2,25,64,128]{3,2,1,0:T(8,128)S(1)} %copy-done.4, f32[25,64,128]{2,1,0:T(8,128)S(1)} %copy-done.1, f32[2,24,64,128]{3,2,1,0:T(8,128)S(1)} %copy-done.10, ...), kind=kLoop, calls=%fused_computation.39 | loop fusion | flops 5734400 | bytes 15499264 | tf_op jit(solution)/shard_map/add | solution.py:77
  81.4 2.2 %collective-permute-start.8 = (f32[2,25,2,128]{3,2,1,0:T(2,128)}, f32[2,25,2,128]{3,2,1,0:T(2,128)}, u32[]{:S(2)}, u32[]{:S(2)}) collective-permute-start(f32[2,25,2,128]{3,2,1,0:T(2,128)} %get-tuple-element.20), channel_id=1, source_target_pairs={{0,1},{1,2},{2,3},{3,4},{4,5},{5,6},{6,7},{8,9},{9,10},{10,11},{11... | collective-permute-start | bytes 153608 | tf_op jit(solution)/shard_map/ppermute | solution.py:26
  83.6 0.9 copy.269
  85.0 2.3 %fusion.32 = (f32[2,25,64,2]{3,2,1,0:T(8,128)}, f32[2,25,64,2]{3,2,1,0:T(8,128)}) fusion(f32[2,25,64,128]{3,2,1,0:T(8,128)S(1)} %get-tuple-element.16), kind=kLoop, calls=%fused_computation.145 | loop fusion | bytes 102400 | tf_op jit(solution)/shard_map/slice | solution.py:25
  87.3 5.2 %collective-permute-start.9 = (f32[2,25,2,128]{3,2,1,0:T(2,128)}, f32[2,25,2,128]{3,2,1,0:T(2,128)}, u32[]{:S(2)}, u32[]{:S(2)}) collective-permute-start(f32[2,25,2,128]{3,2,1,0:T(2,128)} %get-tuple-element.19), channel_id=1, source_target_pairs={{1,0},{2,1},{3,2},{4,3},{5,4},{6,5},{7,6},{9,8},{10,9},{11,10},{12... | collective-permute-start | bytes 153608 | tf_op jit(solution)/shard_map/ppermute | solution.py:27
  93.4 1.8 %reshape.91 = f32[16,1,800]{2,1,0:T(1,128)} reshape(f32[16,1,2,2,8,25]{5,4,3,2,1,0:T(8,128)} %bitcast.281) | data formatting | bytes 102400
  95.2 7.8 %all-to-all-start.2 = ((f32[16,1,800]{2,1,0:T(1,128)}), f32[16,1,800]{2,1,0:T(1,128)S(1)}, u32[]{:S(2)}, u32[]{:S(2)}) async-start(f32[16,1,800]{2,1,0:T(1,128)} %reshape.91), calls=%async_computation.2 | async-start | bytes 114688 | tf_op jit(solution)/shard_map/all_to_all | solution.py:90
  103.0 1.1 add_multiply_fusion.4
  104.1 2.1 %copy.267 = f32[2,25,64,2]{2,3,1,0:T(2,128)S(1)} copy(f32[2,25,64,2]{3,2,1,0:T(8,128)} %get-tuple-element.17) | data formatting | bytes 51200 | tf_op jit(solution)/shard_map/slice | solution.py:25
  106.2 2.0 %copy.265 = f32[2,25,64,2]{2,3,1,0:T(2,128)S(1)} copy(f32[2,25,64,2]{3,2,1,0:T(8,128)} %get-tuple-element.18) | data formatting | bytes 51200 | tf_op jit(solution)/shard_map/slice | solution.py:24
  108.2 1.5 %collective-permute-start.6 = (f32[2,25,64,2]{2,3,1,0:T(2,128)S(1)}, f32[2,25,64,2]{2,3,1,0:T(2,128)S(1)}, u32[]{:S(2)}, u32[]{:S(2)}) collective-permute-start(f32[2,25,64,2]{2,3,1,0:T(2,128)S(1)} %copy.265), channel_id=1, source_target_pairs={{0,8},{8,16},{16,24},{24,32},{32,40},{40,48},{48,56},{56,64},{64,7... | collective-permute-start | bytes 76808 | tf_op jit(solution)/shard_map/ppermute | solution.py:26
  109.7 3.6 %fusion.12 = f32[2,24,64,128]{3,2,1,0:T(8,128)} fusion(f32[2,25,64,128]{3,2,1,0:T(8,128)} %get-tuple-element.15, f32[24,64,128]{2,1,0:T(8,128)S(1)} %copy-done.11), kind=kLoop, calls=%fused_computation.41 | loop fusion | flops 786432 | bytes 5505024 | tf_op jit(solution)/shard_map/mul | solution.py:68
  113.5 1.7 %copy.268 = f32[2,25,64,2]{3,2,1,0:T(8,128)} copy(f32[2,25,64,2]{2,3,1,0:T(2,128)S(1)} %collective-permute-done.7) | data formatting | bytes 51200 | tf_op jit(solution)/shard_map/ppermute | solution.py:27
  115.3 1.8 %copy.266 = f32[2,25,64,2]{3,2,1,0:T(8,128)} copy(f32[2,25,64,2]{2,3,1,0:T(2,128)S(1)} %collective-permute-done.6) | data formatting | bytes 51200 | tf_op jit(solution)/shard_map/ppermute | solution.py:26
  118.2 0.9 reshape.93
  119.0 9.1 %all-to-all-start.3 = ((f32[16,1,800]{2,1,0:T(1,128)}), f32[16,1,800]{2,1,0:T(1,128)S(1)}, u32[]{:S(2)}, u32[]{:S(2)}) async-start(f32[16,1,800]{2,1,0:T(1,128)} %reshape.93), calls=%async_computation.3 | async-start | bytes 114688 | tf_op jit(solution)/shard_map/all_to_all | solution.py:98
  128.1 7.2 %add_multiply_fusion = f32[2,25,64,129]{3,2,1,0:T(8,128)} fusion(f32[2,25,64,128]{3,2,1,0:T(8,128)S(1)} %get-tuple-element.16, f32[2,25,64,2]{3,2,1,0:T(8,128)} %copy.266, f32[2,25,64,2]{3,2,1,0:T(8,128)} %copy.268, f32[25,64,129]{2,1,0:T(8,128)} %get-tuple-element.22, f32[25,64,129]{2,1,0:T(8,128)} %copy-done.6), kind=kLoop, calls=%fused_computation.8 | loop fusion | flops 6604800 | bytes 4992000 | tf_op jit(solution)/shard_map/add | solution.py:58
  137.7 2.7 %add_multiply_fusion.2 = f32[2,25,65,128]{3,2,1,0:T(8,128)S(1)} fusion(f32[2,25,64,128]{3,2,1,0:T(8,128)S(1)} %get-tuple-element.16, f32[2,25,2,128]{3,2,1,0:T(2,128)} %collective-permute-done.8, f32[2,25,2,128]{3,2,1,0:T(2,128)S(1)} %broadcast_select_fusion, f32[25,65,128]{2,1,0:T(8,128)} %get-tuple-element.28, f32[25,65,128]{2,1,0:T(8,128)} %get-tuple-element.27), kind=kLoop, calls=%fused_computation.18 | loop fusion | flops 6656000 | bytes 5068800 | tf_op jit(solution)/shard_map/add | solution.py:58
  140.7 3.2 %fusion.5 = f32[2,25,64,128]{3,2,1,0:T(8,128)S(1)} fusion(f32[2,25,64,128]{3,2,1,0:T(8,128)S(1)} %copy-done.5, f32[2,25,65,128]{3,2,1,0:T(8,128)S(1)} %add_multiply_fusion.2, f32[2,25,64,129]{3,2,1,0:T(8,128)S(1)} %copy-done.7, f32[2,24,64,128]{3,2,1,0:T(8,128)} %fusion.12, f32[25,64,128]{2,1,0:T(8,128)S(1)} %copy-done.2), kind=kLoop, calls=%fused_computation.26 | loop fusion | flops 3686400 | bytes 12222464 | tf_op jit(solution)/shard_map/mul | solution.py:76
  143.9 1.9 %subtract_select_fusion = (f32[25,64,128]{2,1,0:T(8,128)}, f32[25,64,128]{2,1,0:T(8,128)}, f32[25,64,128]{2,1,0:T(8,128)}) fusion(f32[25]{0:T(128)S(1)} %get-tuple-element.31, f32[25]{0:T(128)S(1)} %get-tuple-element.32, s32[64,128]{1,0:T(8,128)S(1)} %copy-done.16, f32[2,25,64,128]{3,2,1,0:T(8,128)S(1)} %fusion.5), kind=kLoop, calls=%fused_computation.51 | loop fusion | flops 3276800 | bytes 4128968 | tf_op jit(solution)/shard_map/mul | solution.py:126
  (107 shorter events, 10.1 us)
Async XLA Ops:
  0.6 9.0 %copy-start.15 = (s32[64,128]{1,0:T(8,128)S(1)}, s32[64,128]{1,0:T(8,128)}, u32[]{:S(2)}) copy-start(s32[64,128]{1,0:T(8,128)} %param.13) | copy-start | bytes 98308
  0.6 9.1 %copy-start.13 = (f32[25,64,128]{2,1,0:T(8,128)S(1)}, f32[25,64,128]{2,1,0:T(8,128)}, u32[]{:S(2)}) copy-start(f32[25,64,128]{2,1,0:T(8,128)} %param.9) | copy-start | bytes 2457604
  2.2 43.0 %collective-permute-start.3 = (f32[25,1,128]{2,1,0:T(1,128)}, f32[25,1,128]{2,1,0:T(1,128)}, u32[]{:S(2)}, u32[]{:S(2)}) collective-permute-start(f32[25,1,128]{2,1,0:T(1,128)} %slice.173), channel_id=1, source_target_pairs={{0,1},{1,2},{2,3},{3,4},{4,5},{5,6},{6,7},{8,9},{9,10},{10,11},{11... | collective-permute-start | bytes 38408 | tf_op jit(solution)/shard_map/ppermute | solution.py:41
  7.1 32.9 %collective-permute-start = (f32[25,64,1]{1,0,2:T(8,128)S(1)}, f32[25,64,1]{1,0,2:T(8,128)}, u32[]{:S(2)}, u32[]{:S(2)}) collective-permute-start(f32[25,64,1]{1,0,2:T(8,128)S(1)} %copy.287), channel_id=1, source_target_pairs={{120,0},{0,8},{8,16},{16,24},{24,32},{32,40},{40,48},{48,56},{56,6... | collective-permute-start | bytes 19208 | tf_op jit(solution)/shard_map/ppermute | solution.py:35
  9.8 26.3 %copy-start = (f32[25,64,128]{2,1,0:T(8,128)}, f32[25,64,128]{2,1,0:T(8,128)S(1)}, u32[]{:S(2)}) copy-start(f32[25,64,128]{2,1,0:T(8,128)S(1)} %fusion.14) | copy-start | bytes 2457604
  14.1 58.0 %collective-permute-start.5 = (f32[2,25,2,128]{3,2,1,0:T(2,128)}, f32[2,25,2,128]{3,2,1,0:T(2,128)}, u32[]{:S(2)}, u32[]{:S(2)}) collective-permute-start(f32[2,25,2,128]{3,2,1,0:T(2,128)} %get-tuple-element.25), channel_id=1, source_target_pairs={{1,0},{2,1},{3,2},{4,3},{5,4},{6,5},{7,6},{9,8},{10,9},{11,10},{12... | collective-permute-start | bytes 153608 | tf_op jit(solution)/shard_map/ppermute | solution.py:27
  18.4 54.6 %collective-permute-start.4 = (f32[2,25,2,128]{3,2,1,0:T(2,128)}, f32[2,25,2,128]{3,2,1,0:T(2,128)}, u32[]{:S(2)}, u32[]{:S(2)}) collective-permute-start(f32[2,25,2,128]{3,2,1,0:T(2,128)} %get-tuple-element.26), channel_id=1, source_target_pairs={{0,1},{1,2},{2,3},{3,4},{4,5},{5,6},{6,7},{8,9},{9,10},{10,11},{11... | collective-permute-start | bytes 153608 | tf_op jit(solution)/shard_map/ppermute | solution.py:26
  22.3 28.6 %all-to-all-start = ((f32[16,1,800]{2,1,0:T(1,128)}), f32[16,1,800]{2,1,0:T(1,128)S(1)}, u32[]{:S(2)}, u32[]{:S(2)}) async-start(f32[16,1,800]{2,1,0:T(1,128)} %reshape.87), calls=%async_computation | async-start | bytes 114688 | tf_op jit(solution)/shard_map/all_to_all | solution.py:90
  34.2 15.0 %collective-permute-start.1 = (f32[2,25,64,2]{2,3,1,0:T(2,128)S(1)}, f32[2,25,64,2]{2,3,1,0:T(2,128)S(1)}, u32[]{:S(2)}, u32[]{:S(2)}) collective-permute-start(f32[2,25,64,2]{2,3,1,0:T(2,128)S(1)} %copy.243), channel_id=1, source_target_pairs={{0,8},{8,16},{16,24},{24,32},{32,40},{40,48},{48,56},{56,64},{64,7... | collective-permute-start | bytes 76808 | tf_op jit(solution)/shard_map/ppermute | solution.py:26
  36.1 1.4 copy-start.3
  37.5 2.0 %copy-start.9 = (f32[2,25,64,2]{3,2,1,0:T(8,128)S(1)}, f32[2,25,64,2]{3,2,1,0:T(8,128)}, u32[]{:S(2)}) copy-start(f32[2,25,64,2]{3,2,1,0:T(8,128)} %get-tuple-element.23) | copy-start | bytes 76804
  40.1 7.3 %collective-permute-start.2 = (f32[2,25,64,2]{2,3,1,0:T(2,128)S(1)}, f32[2,25,64,2]{2,3,1,0:T(2,128)S(1)}, u32[]{:S(2)}, u32[]{:S(2)}) collective-permute-start(f32[2,25,64,2]{2,3,1,0:T(2,128)S(1)} %copy.245), channel_id=1, source_target_pairs={{8,0},{16,8},{24,16},{32,24},{40,32},{48,40},{56,48},{64,56},{72,6... | collective-permute-start | bytes 76808 | tf_op jit(solution)/shard_map/ppermute | solution.py:27
  42.1 3.1 %copy-start.12 = (f32[25,64,128]{2,1,0:T(8,128)S(1)}, f32[25,64,128]{2,1,0:T(8,128)}, u32[]{:S(2)}) copy-start(f32[25,64,128]{2,1,0:T(8,128)} %param.12) | copy-start | bytes 2457604
  45.3 18.3 %copy-start.6 = (f32[25,64,129]{2,1,0:T(8,128)}, f32[25,64,129]{2,1,0:T(8,128)S(1)}, u32[]{:S(2)}) copy-start(f32[25,64,129]{2,1,0:T(8,128)S(1)} %get-tuple-element.21) | copy-start | bytes 2476804
  54.8 15.7 %all-to-all-start.1 = ((f32[16,1,800]{2,1,0:T(1,128)}), f32[16,1,800]{2,1,0:T(1,128)S(1)}, u32[]{:S(2)}, u32[]{:S(2)}) async-start(f32[16,1,800]{2,1,0:T(1,128)} %reshape.89), calls=%async_computation.1 | async-start | bytes 114688 | tf_op jit(solution)/shard_map/all_to_all | solution.py:98
  70.5 2.4 %copy-start.8 = (f32[25,65,128]{2,1,0:T(8,128)S(1)}, f32[25,65,128]{2,1,0:T(8,128)}, u32[]{:S(2)}) copy-start(f32[25,65,128]{2,1,0:T(8,128)} %get-tuple-element.27) | copy-start | bytes 2496004
  73.0 2.6 %copy-start.1 = (f32[25,64,128]{2,1,0:T(8,128)S(1)}, f32[25,64,128]{2,1,0:T(8,128)}, u32[]{:S(2)}) copy-start(f32[25,64,128]{2,1,0:T(8,128)} %copy-done) | copy-start | bytes 2457604
  73.0 2.6 %copy-start.4 = (f32[2,25,64,128]{3,2,1,0:T(8,128)S(1)}, f32[2,25,64,128]{3,2,1,0:T(8,128)}, u32[]{:S(2)}) copy-start(f32[2,25,64,128]{3,2,1,0:T(8,128)} %get-tuple-element.29) | copy-start | bytes 4915204
  73.0 2.6 %copy-start.10 = (f32[2,24,64,128]{3,2,1,0:T(8,128)S(1)}, f32[2,24,64,128]{3,2,1,0:T(8,128)}, u32[]{:S(2)}) copy-start(f32[2,24,64,128]{3,2,1,0:T(8,128)} %fusion.13) | copy-start | bytes 4718596
  81.4 56.2 %collective-permute-start.8 = (f32[2,25,2,128]{3,2,1,0:T(2,128)}, f32[2,25,2,128]{3,2,1,0:T(2,128)}, u32[]{:S(2)}, u32[]{:S(2)}) collective-permute-start(f32[2,25,2,128]{3,2,1,0:T(2,128)} %get-tuple-element.20), channel_id=1, source_target_pairs={{0,1},{1,2},{2,3},{3,4},{4,5},{5,6},{6,7},{8,9},{9,10},{10,11},{11... | collective-permute-start | bytes 153608 | tf_op jit(solution)/shard_map/ppermute | solution.py:26
  85.0 18.0 %copy-start.2 = (f32[25,64,128]{2,1,0:T(8,128)S(1)}, f32[25,64,128]{2,1,0:T(8,128)}, u32[]{:S(2)}) copy-start(f32[25,64,128]{2,1,0:T(8,128)} %copy-done) | copy-start | bytes 2457604
  87.3 49.5 %collective-permute-start.9 = (f32[2,25,2,128]{3,2,1,0:T(2,128)}, f32[2,25,2,128]{3,2,1,0:T(2,128)}, u32[]{:S(2)}, u32[]{:S(2)}) collective-permute-start(f32[2,25,2,128]{3,2,1,0:T(2,128)} %get-tuple-element.19), channel_id=1, source_target_pairs={{1,0},{2,1},{3,2},{4,3},{5,4},{6,5},{7,6},{9,8},{10,9},{11,10},{12... | collective-permute-start | bytes 153608 | tf_op jit(solution)/shard_map/ppermute | solution.py:27
  92.7 0.7 copy-start.14
  95.2 21.8 %all-to-all-start.2 = ((f32[16,1,800]{2,1,0:T(1,128)}), f32[16,1,800]{2,1,0:T(1,128)S(1)}, u32[]{:S(2)}, u32[]{:S(2)}) async-start(f32[16,1,800]{2,1,0:T(1,128)} %reshape.91), calls=%async_computation.2 | async-start | bytes 114688 | tf_op jit(solution)/shard_map/all_to_all | solution.py:90
  104.1 5.6 %copy-start.11 = (f32[24,64,128]{2,1,0:T(8,128)S(1)}, f32[24,64,128]{2,1,0:T(8,128)}, u32[]{:S(2)}) copy-start(f32[24,64,128]{2,1,0:T(8,128)} %add_multiply_fusion.4) | copy-start | bytes 2359300
  108.2 7.1 %collective-permute-start.6 = (f32[2,25,64,2]{2,3,1,0:T(2,128)S(1)}, f32[2,25,64,2]{2,3,1,0:T(2,128)S(1)}, u32[]{:S(2)}, u32[]{:S(2)}) collective-permute-start(f32[2,25,64,2]{2,3,1,0:T(2,128)S(1)} %copy.265), channel_id=1, source_target_pairs={{0,8},{8,16},{16,24},{24,32},{32,40},{40,48},{48,56},{56,64},{64,7... | collective-permute-start | bytes 76808 | tf_op jit(solution)/shard_map/ppermute | solution.py:26
  109.7 3.8 %collective-permute-start.7 = (f32[2,25,64,2]{2,3,1,0:T(2,128)S(1)}, f32[2,25,64,2]{2,3,1,0:T(2,128)S(1)}, u32[]{:S(2)}, u32[]{:S(2)}) collective-permute-start(f32[2,25,64,2]{2,3,1,0:T(2,128)S(1)} %copy.267), channel_id=1, source_target_pairs={{8,0},{16,8},{24,16},{32,24},{40,32},{48,40},{56,48},{64,56},{72,6... | collective-permute-start | bytes 76808 | tf_op jit(solution)/shard_map/ppermute | solution.py:27
  119.0 16.3 %all-to-all-start.3 = ((f32[16,1,800]{2,1,0:T(1,128)}), f32[16,1,800]{2,1,0:T(1,128)S(1)}, u32[]{:S(2)}, u32[]{:S(2)}) async-start(f32[16,1,800]{2,1,0:T(1,128)} %reshape.93), calls=%async_computation.3 | async-start | bytes 114688 | tf_op jit(solution)/shard_map/all_to_all | solution.py:98
  137.7 2.8 %copy-start.5 = (f32[2,25,64,128]{3,2,1,0:T(8,128)S(1)}, f32[2,25,64,128]{3,2,1,0:T(8,128)}, u32[]{:S(2)}) copy-start(f32[2,25,64,128]{3,2,1,0:T(8,128)} %get-tuple-element.15) | copy-start | bytes 4915204
  137.7 3.0 %copy-start.7 = (f32[2,25,64,129]{3,2,1,0:T(8,128)S(1)}, f32[2,25,64,129]{3,2,1,0:T(8,128)}, u32[]{:S(2)}) copy-start(f32[2,25,64,129]{3,2,1,0:T(8,128)} %add_multiply_fusion) | copy-start | bytes 4953604
  140.7 3.2 %copy-start.16 = (s32[64,128]{1,0:T(8,128)S(1)}, s32[64,128]{1,0:T(8,128)}, u32[]{:S(2)}) copy-start(s32[64,128]{1,0:T(8,128)} %param.13) | copy-start | bytes 98308
